TPU v7x, 32 devices: a whole 2x2x4 slice. The times are simulated.
32 devices in a mesh: grp: 2 (over x), chan: 16 (over z, y, core).
Axes of the slice: x: 2, y: 2, z: 4, core: 2. Of those that a mesh axis runs over, the one named last changes fastest.
Arguments:
- samples: bfloat16 [128, 62, 8192], P('chan', 'grp'), parts along dimension 1, may hold values from -6 to 6
- eq_gain: float32 [128, 4096], P('chan'), may hold values from 0.5 to 2
- delays: float32 [1024, 64], replicated, may hold values from -64 to 64
Outputs:
- beams: bfloat16 [2, 1024, 4096], P('grp', 'chan'), parts along dimension 0
There are 2 independent parts, one for each index of `grp`. A program takes and returns all parts, laid end to end along the dimension named above; an argument that names none is the same for every part. Nothing has to cross between parts.
All inputs are finite; a program needn't handle non-finite values.
Results may differ from a plain program's by a relative error of at most 0.0034.
Values may be sent and summed in bfloat16 or wider, within the bound.
No kernel may reach another device: no remote copies, remote signals or barrier semaphores. Data moves between devices by JAX's collectives and lax.ppermute only.
A program may use at most 448 MiB of HBM per device.

v0:
```python
import math

import jax
import jax.numpy as jnp
from jax import lax
from jax.sharding import PartitionSpec as P

DISHES = 64
POLS = 2
NB = 1024
TAPS = 16
AVG = 16
SPEC = 16


def pfb_taps(frame_len, tap_count):
    tap_total = tap_count * frame_len
    position = jnp.arange(tap_total, dtype=jnp.float32) + 0.5
    window = 0.5 - 0.5 * jnp.cos(2.0 * math.pi / tap_total * position)
    offset = (position - 0.5 * tap_total) / frame_len
    prototype = window * jnp.sin(math.pi * offset) / (math.pi * offset)
    prototype = prototype / jnp.sqrt(jnp.sum(prototype * prototype))
    return prototype.reshape(tap_count, frame_len)


def cos_sin(numer, denom):
    phase_angle = 2.0 * math.pi / denom * numer.astype(jnp.float32)
    return (jnp.cos(phase_angle), -jnp.sin(phase_angle))


def turn_tables(frame_len):
    outer_len = 2 ** ((frame_len.bit_length() - 1) // 2)
    inner_len = frame_len // outer_len
    half_len = inner_len // 2
    outer_index = jnp.arange(outer_len, dtype=jnp.int32)
    inner_index = jnp.arange(inner_len, dtype=jnp.int32)
    half_index = jnp.arange(half_len, dtype=jnp.int32)
    one_cos, one_sin = cos_sin(outer_index[:, None] * outer_index[None, :] % outer_len, outer_len)
    twist_cos, twist_sin = cos_sin(
        outer_index[:, None] * inner_index[None, :] % frame_len, frame_len
    )
    three_cos, three_sin = cos_sin(
        inner_index[:, None] * half_index[None, :] % inner_len, inner_len
    )
    table_one = jnp.stack([one_cos, one_sin])
    table_three = jnp.stack([three_cos, three_sin])
    return (outer_len, inner_len, table_one, twist_cos, twist_sin, table_three)


def body(samples, eq_gain, delays):
    inputs_here, frame_count, frame_len = samples.shape
    chan_count = frame_len // 2
    groups = lax.axis_size("chan")
    my_index = lax.axis_index("chan")
    chan_here = chan_count // groups
    beams_here = NB // groups
    time_bins = SPEC // AVG
    highest = lax.Precision.HIGHEST
    tap_table = pfb_taps(frame_len, TAPS)
    filtered = jnp.zeros((inputs_here, SPEC, frame_len), jnp.float32)
    for tap_index in range(TAPS):
        filtered = filtered + tap_table[tap_index] * samples[
            :, tap_index : tap_index + SPEC, :
        ].astype(jnp.float32)
    outer_len, inner_len, table_one, twist_cos, twist_sin, table_three = turn_tables(frame_len)
    framed = filtered.reshape(inputs_here, SPEC, outer_len, inner_len)
    section_one = jnp.einsum("rkn,isnm->irskm", table_one, framed, precision=highest)
    real_one = section_one[:, 0]
    imag_one = section_one[:, 1]
    twisted = jnp.stack(
        [real_one * twist_cos - imag_one * twist_sin, real_one * twist_sin + imag_one * twist_cos],
        axis=1,
    )
    section_three = jnp.einsum("irskm,qmj->irqsjk", twisted, table_three, precision=highest)
    spec_real = (section_three[:, 0, 0] - section_three[:, 1, 1]).reshape(
        inputs_here, SPEC, chan_count
    )
    spec_imag = (section_three[:, 0, 1] + section_three[:, 1, 0]).reshape(
        inputs_here, SPEC, chan_count
    )
    gain_row = eq_gain[:, None, :]
    voltages = jnp.stack(
        [(spec_real * gain_row).astype(jnp.bfloat16), (spec_imag * gain_row).astype(jnp.bfloat16)],
        axis=1,
    )
    row_width = chan_here * inputs_here * 2 * AVG
    outgoing = (
        voltages.reshape(inputs_here, 2, time_bins, AVG, chan_count)
        .transpose(2, 4, 0, 1, 3)
        .reshape(time_bins, groups, row_width)
    )
    channel = (my_index * chan_here + jnp.arange(chan_here, dtype=jnp.int32)).astype(jnp.float32)
    phase_turns = channel[:, None, None] * delays[None, :, :] / frame_len
    phase_angle = 2.0 * math.pi * phase_turns
    weight_scale = 1.0 / math.sqrt(DISHES)
    w_real = (jnp.cos(phase_angle) * weight_scale).astype(jnp.bfloat16)
    w_imag = (-jnp.sin(phase_angle) * weight_scale).astype(jnp.bfloat16)
    weight_stack = jnp.stack(
        [jnp.stack([w_real, -w_imag], axis=-1), jnp.stack([w_imag, w_real], axis=-1)], axis=1
    )
    block_count = math.gcd(chan_here, 8)
    block_len = chan_here // block_count
    weight_blocks = weight_stack.reshape(block_count, block_len, 2, NB, DISHES, 2)
    arrived = lax.all_to_all(outgoing, "chan", split_axis=1, concat_axis=1, tiled=True)
    item_count = arrived.shape[0]
    volt_grid = arrived.reshape(item_count, groups, chan_here, inputs_here, 2, AVG)
    volt_grid = volt_grid.transpose(2, 1, 3, 4, 0, 5).reshape(
        block_count, block_len, DISHES, POLS, 2, item_count, AVG
    )

    def one_block(block_pair):
        weight_part, volt_part = block_pair
        product = jnp.einsum(
            "cobdr,cdprqa->cobpqa", weight_part, volt_part, preferred_element_type=jnp.float32
        )
        return jnp.sum(product * product, axis=(1, 3, 5)) / AVG

    energy = lax.map(one_block, (weight_blocks, volt_grid))
    power_bins = energy.reshape(chan_here, NB, item_count).transpose(2, 1, 0).astype(jnp.bfloat16)
    sending = power_bins.reshape(item_count, groups, beams_here * chan_here)
    landed = lax.all_to_all(sending, "chan", split_axis=1, concat_axis=1, tiled=True)
    return (
        landed.reshape(time_bins, groups, beams_here, chan_here)
        .transpose(0, 2, 1, 3)
        .reshape(time_bins, beams_here, chan_count)
    )


def solution(mesh):
    in_specs = (P("chan", "grp", None), P("chan", None), P())
    out_specs = P("grp", "chan", None)
    return jax.shard_map(body, mesh=mesh, in_specs=in_specs, out_specs=out_specs, check_vma=False)
```

profile of v0, /device:TPU:0, one launch (start us, length us, event | category | flops | bytes accessed | tf_op | source)
XLA Modules:
  0.0 907.0 jit_solution(4844415604220031745)
XLA Ops:
  0.0 0.1 sine_negate_fusion.2
  0.1 4.2 fusion.34
  4.4 0.1 sine_negate_fusion.1
  4.5 0.1 sine_negate_fusion
  5.4 3.6 fusion.29
  9.0 16.8 %add_bitcast_fusion = f32[8,16,64,128,1]{3,0,2,1,4:T(8,128)S(1)} fusion(bf16[8,31,8192]{2,0,1:T(8,128)(2,1)} %param.5, f32[8192]{0:T(1024)S(1)} %get-tuple-element.53, f32[8192]{0:T(1024)S(1)} %get-tuple-element.54, f32[8192]{0:T(1024)S(1)} %get-tuple-element.55, f32[8192]{0:T(1024)S(1)} %get-tuple-element.56, f32[8192]{0:T(1024)S(1)} %get-tuple-element.57, ...), kind=kLoop, calls=%fused_computation.26 | loop fusion | flops 49283072 | bytes 38273024 | tf_op jit(solution)/shard_map/reshape | solution.py:66
  25.8 7.2 fusion.18
  33.1 2.0 multiply_subtract_fusion
  35.1 27.6 %fusion.12 = f32[8,2,2,16,64,64]{5,4,3,1,0,2:T(8,128)} fusion(f32[1,128,64]{1,2,0:T(8,128)S(1)} %get-tuple-element.76, f32[1,128,64]{1,2,0:T(8,128)S(1)} %get-tuple-element.77, f32[8,1,16,64,128]{4,3,1,2,0:T(8,128)S(1)} %get-tuple-element.51, f32[8,1,16,64,128]{4,3,1,2,0:T(8,128)S(1)} %get-tuple-element.50), kind=kOutput, calls=%fused_computation.18 | convolution fusion | flops 3223339008 | bytes 16842752 | tf_op jit(solution)/shard_map/irskm,qmj->irqsjk/dot_general | solution.py:74
  62.7 12.0 %slice_subtract_fusion = (f32[8,1,1,16,64,64]{5,4,3,1,0,2:T(8,128)}, f32[8,1,1,16,64,64]{5,4,3,1,0,2:T(8,128)}) fusion(f32[8,2,2,16,64,64]{5,4,3,1,0,2:T(8,128)} %fusion.12), kind=kLoop, calls=%fused_computation.21 | loop fusion | flops 1048576 | bytes 12582912 | tf_op jit(solution)/shard_map/sub | solution.py:75
  74.7 3.5 sub.38
  78.2 4.8 add.166
  83.1 1.9 fusion.22
  85.0 0.2 maximum_bitcast_fusion
  85.2 27.8 %copy.27 = bf16[1,4096,8,2,16]{4,3,2,1,0:T(2,128)(2,1)} copy(bf16[1,4096,8,2,16]{1,4,3,2,0:T(8,128)(2,1)S(1)} %maximum_bitcast_fusion) | data formatting | bytes 4194304 | tf_op jit(solution)/shard_map/transpose | solution.py:89
  113.1 18.3 %reshape.393 = bf16[1,16,65536]{2,0,1:T(2,128)(2,1)} reshape(bf16[1,4096,8,2,16]{4,3,2,1,0:T(2,128)(2,1)} %copy.27) | data formatting | bytes 4194304 | tf_op jit(solution)/shard_map/reshape | solution.py:90
  131.4 0.5 broadcast.400
  132.0 13.0 %reduce.6 = bf16[16,65536]{1,0:T(8,128)(2,1)S(1)} reduce(bf16[16,1,65536]{2,1,0:T(2,128)(2,1)} %bitcast.92, bf16[]{:T(256)} %broadcast.400), dimensions={1}, to_apply=%bitcast.78.reduce_sub_computation | reduce | bytes 4194306
  144.9 2.9 reshape.397
  147.9 7.4 all-to-all-start
  155.4 251.5 %multiply_convert_fusion = (bf16[8,32,1,1024,64,1]{3,4,5,2,1,0:T(8,128)(2,1)}, bf16[8,32,1,1024,64,1]{3,4,5,2,1,0:T(8,128)(2,1)}) fusion(f32[1024,64]{0,1:T(8,128)S(1)} %copy-done, f32[8,32]{1,0:T(8,128)S(1)} %add_convert_fusion), kind=kLoop, calls=%fused_computation.11 | loop fusion | flops 117440512 | bytes 67372032 | tf_op jit(solution)/shard_map/convert_element_type | solution.py:97
  406.8 229.4 %fusion.15 = bf16[8,32,1,1024,64,1]{3,4,5,2,1,0:T(8,128)(2,1)} fusion(f32[1024,64]{0,1:T(8,128)S(1)} %copy-done, f32[8,32]{1,0:T(8,128)S(1)} %add_convert_fusion), kind=kLoop, calls=%fused_computation.19 | loop fusion | flops 134217728 | bytes 33817600 | tf_op jit(solution)/shard_map/neg | solution.py:99
  636.2 86.9 %maximum_maximum_fusion = bf16[8,32,2,1024,64,2]{3,4,5,2,1,0:T(8,128)(2,1)} fusion(bf16[8,32,1,1024,64,1]{3,4,5,2,1,0:T(8,128)(2,1)} %get-tuple-element.69, bf16[8,32,1,1024,64,1]{3,4,5,2,1,0:T(8,128)(2,1)} %get-tuple-element.68, bf16[8,32,1,1024,64,1]{3,4,5,2,1,0:T(8,128)(2,1)} %fusion.15), kind=kLoop, calls=%fused_computation.10 | loop fusion | flops 201326592 | bytes 234881024 | tf_op jit(solution)/shard_map/stack | solution.py:98
  723.2 6.8 reshape.398
  729.9 13.2 %bitcast_reduce_fusion = bf16[16,65536]{1,0:T(8,128)(2,1)S(1)} fusion(bf16[16,1,65536]{2,1,0:T(2,128)(2,1)} %reshape.398), kind=kLoop, calls=%fused_computation.91 | loop fusion | bytes 4194304 | tf_op jit(solution)/shard_map/all_to_all | solution.py:104
  743.1 20.1 %reshape.381 = bf16[1,16,256,8,2,16]{5,4,3,2,1,0:T(2,128)(2,1)} reshape(bf16[16,65536]{1,0:T(8,128)(2,1)S(1)} %bitcast_reduce_fusion) | data formatting | bytes 4194304 | tf_op jit(solution)/shard_map/reshape | solution.py:106
  763.3 35.2 %copy.29 = bf16[256,16,8,2,1,16]{0,5,3,2,1,4:T(8,128)(2,1)S(1)} copy(bf16[256,16,8,2,1,16]{5,3,2,0,1,4:T(2,128)(2,1)} %bitcast.91) | data formatting | bytes 4194304 | tf_op jit(solution)/shard_map/transpose | solution.py:107
  798.5 6.2 reshape.382
  804.7 13.3 %copy.30 = bf16[8,32,64,2,2,1,16]{2,6,4,3,1,5,0:T(8,128)(2,1)} copy(bf16[8,32,64,2,2,1,16]{1,0,6,4,3,2,5:T(8,128)(2,1)} %reshape.382) | data formatting | bytes 4194304 | tf_op jit(solution)/shard_map/while | solution.py:118
  818.0 59.0 %while.10 = (s32[]{:T(128)}, bf16[8,32,1024,1]{2,3,1,0:T(2,128)(2,1)S(1)}, bf16[8,32,2,1024,64,2]{3,4,5,2,1,0:T(8,128)(2,1)}, bf16[8,32,64,2,2,1,16]{2,6,4,3,1,5,0:T(8,128)(2,1)}, s32[]{:T(128)}) while((s32[]{:T(128)}, bf16[8,32,1024,1]{2,3,1,0:T(2,128)(2,1)S(1)}, bf16[8,32,2,1024,64,2]{3,4,5,2,1,0:T(8,128)(2,1)}, ...), condition=%wide.region_3.4_spmd, body=%wide.region_1.3_spmd.sunk | while | flops 541097984 | bytes 17826888 | solution.py:118
  818.0 7.2 fusion.68
  825.3 7.2 fusion.68
  832.7 7.3 fusion.68
  840.1 7.3 fusion.68
  847.5 7.2 fusion.68
  854.9 7.2 fusion.68
  862.2 7.3 fusion.68
  869.6 7.3 fusion.68
  877.0 0.2 copy.42
  877.2 0.2 copy.31
  877.4 0.5 reshape.394
  877.9 3.7 reduce.7
  881.6 0.4 reshape.399
  882.0 20.3 %all_to_all.10 = bf16[16,2,8192]{2,1,0:T(2,128)(2,1)S(1)} all-to-all(bf16[16,2,8192]{2,1,0:T(2,128)(2,1)S(1)} %reshape.399), channel_id=1, replica_groups=mesh['grp'=2,'chan'=16] {'chan'}, dimensions={0} | all-to-all | bytes 1048576 | tf_op jit(solution)/shard_map/all_to_all | solution.py:121
  902.3 0.5 reshape.400
  902.8 3.0 bitcast_reduce_fusion.1
  905.8 0.1 copy.44
  906.0 0.8 copy.43
  (25 shorter events, 0.9 us)
Async XLA Ops:
  78.2 4.8 copy-start.1
  144.9 10.4 %copy-start = (f32[1024,64]{0,1:T(8,128)S(1)}, f32[1024,64]{0,1:T(8,128)}, u32[]{:S(2)}) copy-start(f32[1024,64]{0,1:T(8,128)} %param.7) | copy-start | bytes 786436
  147.9 575.3 %all-to-all-start = ((bf16[16,2,32768]{2,1,0:T(2,128)(2,1)}), bf16[16,2,32768]{2,1,0:T(2,128)(2,1)S(1)}, u32[]{:S(2)}, u32[]{:S(2)}) async-start(bf16[16,2,32768]{2,1,0:T(2,128)(2,1)} %reshape.397), calls=%async_computation | async-start | bytes 4194304 | tf_op jit(solution)/shard_map/all_to_all | solution.py:104
where the time goes:
time: 916 us; the launch traced here: 907 us
  other arithmetic  626 us (68%)
  local copies, waits for them, and re-layouts  159 us (17%)
  matrix products  92.8 us (10%)
  blocking collectives  20.3 us (2%)
    convert_element_type x1, other arithmetic, body(): w_imag = (-jnp.sin(phase_angle) * weight_scale).astype(jnp.bfloat16)  251 us
    neg x1, other arithmetic, body(): -w_imag  229 us
    another operation x1, other arithmetic, body(): jnp.stack([jnp.stack([w_real, -w_imag], axis=-1), jnp.stack([w_imag, w_re...  86.9 us
    dot_general x8, matrix products, one_block(): jnp.einsum('cobdr,cdprqa->cobpqa', weight_part, volt_part, preferred_elem...  58 us
    transpose x1, local copies, waits for them, and re-layouts, body(): volt_grid.transpose(2, 1, 3, 4, 0, 5)  35.2 us
    transpose x1, local copies, waits for them, and re-layouts, body(): outgoing = voltages.reshape(inputs_here, 2, time_bins, AVG, chan_count).t...  27.8 us
    dot_general x1, matrix products, body(): jnp.einsum('irskm,qmj->irqsjk', twisted, table_three, precision=highest)  27.6 us
    all_to_all x1, blocking collectives, body(): lax.all_to_all(sending, 'chan', split_axis=1, concat_axis=1, tiled=True)  20.3 us
  transfers between devices with their start and end apart: 1, of which 0 were waited for; matrix products, arithmetic and copies ran while one was open for 63% of the time, Pallas kernels for 0%

commit v1 on v0

--- a/solution.py
+++ b/solution.py
@@ -79,51 +79,50 @@
         inputs_here, SPEC, chan_count
     )
     gain_row = eq_gain[:, None, :]
-    voltages = jnp.stack(
-        [(spec_real * gain_row).astype(jnp.bfloat16), (spec_imag * gain_row).astype(jnp.bfloat16)],
+    volt_real = (spec_real * gain_row).astype(jnp.bfloat16)
+    volt_imag = (spec_imag * gain_row).astype(jnp.bfloat16)
+    outgoing = jnp.stack([volt_real, volt_imag], axis=1).transpose(3, 1, 2, 0)
+    arrived = lax.all_to_all(outgoing, "chan", split_axis=0, concat_axis=3, tiled=True)
+    dish_volts = arrived.reshape(chan_here, 2, SPEC, DISHES, POLS).transpose(0, 1, 4, 2, 3)
+    real_part = dish_volts[:, 0]
+    imag_part = dish_volts[:, 1]
+    volt_operand = jnp.stack(
+        [
+            jnp.concatenate([real_part, -imag_part], axis=-1),
+            jnp.concatenate([imag_part, real_part], axis=-1),
+        ],
         axis=1,
+    ).reshape(chan_here, 2 * POLS * SPEC, 2 * DISHES)
+    low_len = math.gcd(chan_here, 2 ** ((chan_here.bit_length() - 1) // 2))
+    high_count = chan_here // low_len
+    weight_scale = 1.0 / math.sqrt(DISHES)
+
+    def rotation(channel, scale):
+        turns = channel.astype(jnp.float32)[:, None, None] * delays[None, :, :] / frame_len
+        turns = turns - jnp.round(turns)
+        angle = 2.0 * math.pi * turns
+        return jnp.cos(angle) * scale, -jnp.sin(angle) * scale
+
+    high_channel = my_index * chan_here + jnp.arange(high_count, dtype=jnp.int32) * low_len
+    high_real, high_imag = rotation(high_channel, weight_scale)
+    low_real, low_imag = rotation(jnp.arange(low_len, dtype=jnp.int32), 1.0)
+    volt_blocks = volt_operand.reshape(high_count, low_len, 2 * POLS * SPEC, 2 * DISHES)
+
+    def one_block(block_args):
+        base_real, base_imag, volt_part = block_args
+        w_real = (base_real * low_real - base_imag * low_imag).astype(jnp.bfloat16)
+        w_imag = (base_real * low_imag + base_imag * low_real).astype(jnp.bfloat16)
+        weight_part = jnp.concatenate([w_real, w_imag], axis=-1)
+        product = jnp.einsum(
+            "cnk,cbk->cnb", volt_part, weight_part, preferred_element_type=jnp.float32
+        ).reshape(low_len, 2 * POLS, time_bins, AVG, NB)
+        return jnp.sum(product * product, axis=(1, 3)) / AVG
+
+    energy = lax.map(one_block, (high_real, high_imag, volt_blocks))
+    power_bins = (
+        energy.reshape(chan_here, time_bins, NB).transpose(1, 2, 0).astype(jnp.bfloat16)
     )
-    row_width = chan_here * inputs_here * 2 * AVG
-    outgoing = (
-        voltages.reshape(inputs_here, 2, time_bins, AVG, chan_count)
-        .transpose(2, 4, 0, 1, 3)
-        .reshape(time_bins, groups, row_width)
-    )
-    channel = (my_index * chan_here + jnp.arange(chan_here, dtype=jnp.int32)).astype(jnp.float32)
-    phase_turns = channel[:, None, None] * delays[None, :, :] / frame_len
-    phase_angle = 2.0 * math.pi * phase_turns
-    weight_scale = 1.0 / math.sqrt(DISHES)
-    w_real = (jnp.cos(phase_angle) * weight_scale).astype(jnp.bfloat16)
-    w_imag = (-jnp.sin(phase_angle) * weight_scale).astype(jnp.bfloat16)
-    weight_stack = jnp.stack(
-        [jnp.stack([w_real, -w_imag], axis=-1), jnp.stack([w_imag, w_real], axis=-1)], axis=1
-    )
-    block_count = math.gcd(chan_here, 8)
-    block_len = chan_here // block_count
-    weight_blocks = weight_stack.reshape(block_count, block_len, 2, NB, DISHES, 2)
-    arrived = lax.all_to_all(outgoing, "chan", split_axis=1, concat_axis=1, tiled=True)
-    item_count = arrived.shape[0]
-    volt_grid = arrived.reshape(item_count, groups, chan_here, inputs_here, 2, AVG)
-    volt_grid = volt_grid.transpose(2, 1, 3, 4, 0, 5).reshape(
-        block_count, block_len, DISHES, POLS, 2, item_count, AVG
-    )
-
-    def one_block(block_pair):
-        weight_part, volt_part = block_pair
-        product = jnp.einsum(
-            "cobdr,cdprqa->cobpqa", weight_part, volt_part, preferred_element_type=jnp.float32
-        )
-        return jnp.sum(product * product, axis=(1, 3, 5)) / AVG
-
-    energy = lax.map(one_block, (weight_blocks, volt_grid))
-    power_bins = energy.reshape(chan_here, NB, item_count).transpose(2, 1, 0).astype(jnp.bfloat16)
-    sending = power_bins.reshape(item_count, groups, beams_here * chan_here)
-    landed = lax.all_to_all(sending, "chan", split_axis=1, concat_axis=1, tiled=True)
-    return (
-        landed.reshape(time_bins, groups, beams_here, chan_here)
-        .transpose(0, 2, 1, 3)
-        .reshape(time_bins, beams_here, chan_count)
-    )
+    return lax.all_to_all(power_bins, "chan", split_axis=1, concat_axis=2, tiled=True)
 
 
 def solution(mesh):

time: 916 us -> 584 us (0.64)
  other arithmetic: 626 us -> 336 us
  local copies, waits for them, and re-layouts: 159 us -> 116 us
  matrix products: 92.8 us -> 63.1 us
  waiting for transfers between devices: 0.01 us -> 24 us
    neg x1, other arithmetic: 229 us -> 0.07 us  [body(): -imag_part]
    another operation x1 -> x3, other arithmetic: 86.9 us -> 2.85 us  [the longest x2 2.66 us: body(): jnp.stack([jnp.concatenate([real_part, -imag_part], axis=-1), jnp.concate...]
    transpose x2 -> x0, local copies, waits for them, and re-layouts: 63 us -> none  [the longest x1 35.2 us: body(): volt_grid.transpose(2, 1, 3, 4, 0, 5)]
    reshape x5 -> x0, local copies, waits for them, and re-layouts: 46 us -> none  [the longest x1 20.1 us: body(): arrived.reshape(item_count, groups, chan_here, inputs_here, 2, AVG)]
    unnamed x12 -> x11, local copies, waits for them, and re-layouts: 11.5 us -> 50.9 us
    dot_general x8 -> x16, matrix products: 58 us -> 28 us  [one_block(): jnp.einsum('cnk,cbk->cnb', volt_part, weight_part, preferred_element_type...]
    all_to_all x1, waiting for transfers between devices: 0.01 us -> 24 us  [body(): lax.all_to_all(outgoing, 'chan', split_axis=0, concat_axis=3, tiled=True)]
    another operation x0 -> x2, local copies, waits for them, and re-layouts: none -> 23.1 us  [the longest x1 14 us: body(): outgoing = jnp.stack([volt_real, volt_imag], axis=1).transpose(3, 1, 2, 0)]
  transfers between devices with their start and end apart: 1 -> 1, of which waited for: 0 -> 1; matrix products, arithmetic and copies ran while one was open for 63% -> 3% of each run, Pallas kernels for 0% -> 0%
where the time goes in v1:
time: 584 us; the launch traced here: 574 us
  other arithmetic  336 us (58%)
  local copies, waits for them, and re-layouts  116 us (20%)
  matrix products  63.1 us (11%)
  blocking collectives  25.5 us (4%)
  waiting for transfers between devices  24 us (4%)
  starting transfers between devices  7.64 us (1%)
    convert_element_type x16, other arithmetic, one_block(): w_real = (base_real * low_real - base_imag * low_imag).astype(jnp.bfloat16)  272 us
    unnamed x11, local copies, waits for them, and re-layouts  50.9 us
    dot_general x16, matrix products, one_block(): jnp.einsum('cnk,cbk->cnb', volt_part, weight_part, preferred_element_type...  28 us
    dot_general x1, matrix products, body(): jnp.einsum('irskm,qmj->irqsjk', twisted, table_three, precision=highest)  27.9 us
    all_to_all x1, blocking collectives, body(): lax.all_to_all(power_bins, 'chan', split_axis=1, concat_axis=2, tiled=True)  25.5 us
    all_to_all x1, waiting for transfers between devices, body(): lax.all_to_all(outgoing, 'chan', split_axis=0, concat_axis=3, tiled=True)  24 us
    mul x16, local copies, waits for them, and re-layouts, one_block(): w_real = (base_real * low_real - base_imag * low_imag).astype(jnp.bfloat16)  17.1 us
    mul x1, other arithmetic, rotation(): return (jnp.cos(angle) * scale, -jnp.sin(angle) * scale)  17 us
  transfers between devices with their start and end apart: 1, of which 1 were waited for; matrix products, arithmetic and copies ran while one was open for 3% of the time, Pallas kernels for 0%

profile of v1, /device:TPU:0, one launch (start us, length us, event | category | flops | bytes accessed | tf_op | source)
XLA Modules:
  0.0 574.4 jit_solution(7906501570208651804)
XLA Ops:
  0.0 4.2 fusion.49
  5.4 3.6 fusion.44
  9.0 16.5 %add_bitcast_fusion = f32[8,16,64,128,1]{3,0,2,1,4:T(8,128)S(1)} fusion(bf16[8,31,8192]{2,0,1:T(8,128)(2,1)} %param.5, f32[8192]{0:T(1024)S(1)} %get-tuple-element.151, f32[8192]{0:T(1024)S(1)} %get-tuple-element.152, f32[8192]{0:T(1024)S(1)} %get-tuple-element.153, f32[8192]{0:T(1024)S(1)} %get-tuple-element.154, f32[8192]{0:T(1024)S(1)} %get-tuple-element.155, ...), kind=kLoop, calls=%fused_computation.42 | loop fusion | flops 49283072 | bytes 38273024 | tf_op jit(solution)/shard_map/reshape | solution.py:66
  25.5 7.2 %fusion.33 = f32[8,2,16,64,128]{4,3,1,2,0:T(8,128)S(1)} fusion(f32[8,16,64,128,1]{3,0,2,1,4:T(8,128)S(1)} %add_bitcast_fusion, f32[1,64,64]{2,1,0:T(8,128)S(1)} %get-tuple-element.170, f32[1,64,64]{2,1,0:T(8,128)S(1)} %get-tuple-element.171), kind=kOutput, calls=%fused_computation.43 | convolution fusion | flops 1610620928 | bytes 12615680 | tf_op jit(solution)/shard_map/rkn,isnm->irskm/dot_general | solution.py:67
  32.8 2.0 multiply_subtract_fusion
  34.8 27.9 %fusion.27 = f32[8,2,2,16,64,64]{5,4,3,1,0,2:T(8,128)} fusion(f32[1,128,64]{1,2,0:T(8,128)S(1)} %get-tuple-element.174, f32[1,128,64]{1,2,0:T(8,128)S(1)} %get-tuple-element.175, f32[8,1,16,64,128]{4,3,1,2,0:T(8,128)S(1)} %get-tuple-element.145, f32[8,1,16,64,128]{4,3,1,2,0:T(8,128)S(1)} %get-tuple-element.144), kind=kOutput, calls=%fused_computation.30 | convolution fusion | flops 3223339008 | bytes 16842752 | tf_op jit(solution)/shard_map/irskm,qmj->irqsjk/dot_general | solution.py:74
  62.7 12.1 %slice_subtract_fusion = (f32[8,1,1,16,64,64]{5,4,3,1,0,2:T(8,128)}, f32[8,1,1,16,64,64]{5,4,3,1,0,2:T(8,128)}) fusion(f32[8,2,2,16,64,64]{5,4,3,1,0,2:T(8,128)} %fusion.27), kind=kLoop, calls=%fused_computation.34 | loop fusion | flops 1048576 | bytes 12582912 | tf_op jit(solution)/shard_map/sub | solution.py:75
  74.8 3.5 add.165
  78.3 4.8 sub.47
  83.1 1.9 fusion.37
  85.3 14.0 %copy.57 = bf16[8,2,16,4096]{2,0,1,3:T(8,128)(2,1)} copy(bf16[8,2,16,4096]{3,2,1,0:T(8,128)(2,1)S(1)} %pad_maximum_fusion.2) | data formatting | bytes 4194304 | tf_op jit(solution)/shard_map/stack | solution.py:84
  99.3 14.5 %bitcast_bitcast_fusion = bf16[4096,2,8,16]{3,2,1,0:T(8,128)(2,1)} fusion(bf16[8,2,16,4096]{2,0,1,3:T(8,128)(2,1)} %copy.57), kind=kLoop, calls=%fused_computation.112 | loop fusion | bytes 4194304
  113.8 20.8 %reshape.329 = bf16[16,2,32768]{2,1,0:T(2,128)(2,1)} reshape(bf16[4096,2,8,16]{3,2,1,0:T(8,128)(2,1)} %bitcast_bitcast_fusion) | data formatting | bytes 4194304
  134.6 7.6 %all-to-all-start = ((bf16[16,2,32768]{2,1,0:T(2,128)(2,1)}), bf16[16,2,32768]{2,1,0:T(2,128)(2,1)S(1)}, u32[]{:S(2)}, u32[]{:S(2)}) async-start(bf16[16,2,32768]{2,1,0:T(2,128)(2,1)} %reshape.329), calls=%async_computation | async-start | bytes 4194304 | tf_op jit(solution)/shard_map/all_to_all | solution.py:85
  142.2 17.0 %negate_multiply_fusion = (f32[16,1024,64]{1,2,0:T(8,128)}, f32[16,1024,64]{1,2,0:T(8,128)}) fusion(f32[1024,64]{0,1:T(8,128)S(1)} %copy-done, f32[16]{0:T(128)S(1)} %add_convert_fusion), kind=kLoop, calls=%fused_computation.38 | loop fusion | flops 8388608 | bytes 8650816 | tf_op jit(solution)/shard_map/mul | solution.py:104
  159.3 24.0 %all-to-all-done = bf16[16,2,32768]{2,1,0:T(2,128)(2,1)S(1)} async-done(((bf16[16,2,32768]{2,1,0:T(2,128)(2,1)}), bf16[16,2,32768]{2,1,0:T(2,128)(2,1)S(1)}, u32[]{:S(2)}, u32[]{:S(2)}) %all-to-all-start) | async-done | bytes 2097184 | tf_op jit(solution)/shard_map/all_to_all | solution.py:85
  183.3 14.4 %reshape.330 = bf16[4096,2,8,16]{3,2,1,0:T(8,128)(2,1)} reshape(bf16[16,2,32768]{2,1,0:T(2,128)(2,1)S(1)} %all-to-all-done) | data formatting | bytes 4194304
  197.7 14.6 %copy.59 = bf16[256,2,16,16,8]{0,2,4,3,1:T(8,128)(2,1)S(1)} copy(bf16[256,2,16,16,8]{2,4,1,0,3:T(8,128)(2,1)} %bitcast.87) | data formatting | bytes 4194304 | tf_op jit(solution)/shard_map/all_to_all | solution.py:85
  212.9 2.3 pad_maximum_fusion.1
  215.2 9.0 %copy.60 = bf16[256,2,2,16,128]{4,3,2,1,0:T(8,128)(2,1)} copy(bf16[256,2,2,16,128]{0,3,2,4,1:T(8,128)(2,1)} %pad_maximum_fusion.1) | data formatting | bytes 8388608 | tf_op jit(solution)/shard_map/stack | solution.py:89
  224.2 317.5 %while.12 = (s32[]{:T(128)}, bf16[16,16,1,1024]{3,1,0,2:T(8,128)(2,1)S(1)}, bf16[16,16,64,128]{3,2,1,0:T(8,128)(2,1)}, f32[16,1024,64]{1,2,0:T(8,128)}, f32[16,1...) while((s32[]{:T(128)}, ...), condition=%wide.region_3.4_spmd.clone.clone, body=%wide.region_1.3_spmd.clone.clone.sunk | while | flops 293601280 | bytes 10683037 | solution.py:121
  225.3 17.0 %fusion.84 = (bf16[16,1024,64]{1,2,0:T(8,128)(2,1)S(1)}, bf16[16,1024,64]{1,2,0:T(8,128)(2,1)S(1)}) fusion(f32[1024,64]{0,1:T(8,128)S(1)} %get-tuple-element.248, f32[16]{0:T(128)S(1)} %get-tuple-element.249, f32[1024,64]{0,1:T(8,128)S(1)} %get-tuple-element.223, f32[1024,64]{0,1:T(8,128)S(1)} %get-tuple-element.224), kind=kLoop, calls=%fused_computation.15.clone.1 | loop fusion | flops 14680064 | bytes 4980800 | tf_op jit(solution)/shard_map/while/body/eval_jaxpr/convert_element_type | solution.py:113
  242.3 1.7 multiply_reduce_fusion.2
  245.1 17.0 %fusion.84 = (bf16[16,1024,64]{1,2,0:T(8,128)(2,1)S(1)}, bf16[16,1024,64]{1,2,0:T(8,128)(2,1)S(1)}) fusion(f32[1024,64]{0,1:T(8,128)S(1)} %get-tuple-element.248, f32[16]{0:T(128)S(1)} %get-tuple-element.249, f32[1024,64]{0,1:T(8,128)S(1)} %get-tuple-element.223, f32[1024,64]{0,1:T(8,128)S(1)} %get-tuple-element.224), kind=kLoop, calls=%fused_computation.15.clone.1 | loop fusion | flops 14680064 | bytes 4980800 | tf_op jit(solution)/shard_map/while/body/eval_jaxpr/convert_element_type | solution.py:113
  262.1 1.7 multiply_reduce_fusion.2
  265.0 17.0 %fusion.84 = (bf16[16,1024,64]{1,2,0:T(8,128)(2,1)S(1)}, bf16[16,1024,64]{1,2,0:T(8,128)(2,1)S(1)}) fusion(f32[1024,64]{0,1:T(8,128)S(1)} %get-tuple-element.248, f32[16]{0:T(128)S(1)} %get-tuple-element.249, f32[1024,64]{0,1:T(8,128)S(1)} %get-tuple-element.223, f32[1024,64]{0,1:T(8,128)S(1)} %get-tuple-element.224), kind=kLoop, calls=%fused_computation.15.clone.1 | loop fusion | flops 14680064 | bytes 4980800 | tf_op jit(solution)/shard_map/while/body/eval_jaxpr/convert_element_type | solution.py:113
  281.9 1.7 multiply_reduce_fusion.2
  284.8 17.0 %fusion.84 = (bf16[16,1024,64]{1,2,0:T(8,128)(2,1)S(1)}, bf16[16,1024,64]{1,2,0:T(8,128)(2,1)S(1)}) fusion(f32[1024,64]{0,1:T(8,128)S(1)} %get-tuple-element.248, f32[16]{0:T(128)S(1)} %get-tuple-element.249, f32[1024,64]{0,1:T(8,128)S(1)} %get-tuple-element.223, f32[1024,64]{0,1:T(8,128)S(1)} %get-tuple-element.224), kind=kLoop, calls=%fused_computation.15.clone.1 | loop fusion | flops 14680064 | bytes 4980800 | tf_op jit(solution)/shard_map/while/body/eval_jaxpr/convert_element_type | solution.py:113
  304.6 17.0 %fusion.84 = (bf16[16,1024,64]{1,2,0:T(8,128)(2,1)S(1)}, bf16[16,1024,64]{1,2,0:T(8,128)(2,1)S(1)}) fusion(f32[1024,64]{0,1:T(8,128)S(1)} %get-tuple-element.248, f32[16]{0:T(128)S(1)} %get-tuple-element.249, f32[1024,64]{0,1:T(8,128)S(1)} %get-tuple-element.223, f32[1024,64]{0,1:T(8,128)S(1)} %get-tuple-element.224), kind=kLoop, calls=%fused_computation.15.clone.1 | loop fusion | flops 14680064 | bytes 4980800 | tf_op jit(solution)/shard_map/while/body/eval_jaxpr/convert_element_type | solution.py:113
  321.6 1.7 multiply_reduce_fusion.2
  324.5 17.0 %fusion.84 = (bf16[16,1024,64]{1,2,0:T(8,128)(2,1)S(1)}, bf16[16,1024,64]{1,2,0:T(8,128)(2,1)S(1)}) fusion(f32[1024,64]{0,1:T(8,128)S(1)} %get-tuple-element.248, f32[16]{0:T(128)S(1)} %get-tuple-element.249, f32[1024,64]{0,1:T(8,128)S(1)} %get-tuple-element.223, f32[1024,64]{0,1:T(8,128)S(1)} %get-tuple-element.224), kind=kLoop, calls=%fused_computation.15.clone.1 | loop fusion | flops 14680064 | bytes 4980800 | tf_op jit(solution)/shard_map/while/body/eval_jaxpr/convert_element_type | solution.py:113
  344.3 17.0 %fusion.84 = (bf16[16,1024,64]{1,2,0:T(8,128)(2,1)S(1)}, bf16[16,1024,64]{1,2,0:T(8,128)(2,1)S(1)}) fusion(f32[1024,64]{0,1:T(8,128)S(1)} %get-tuple-element.248, f32[16]{0:T(128)S(1)} %get-tuple-element.249, f32[1024,64]{0,1:T(8,128)S(1)} %get-tuple-element.223, f32[1024,64]{0,1:T(8,128)S(1)} %get-tuple-element.224), kind=kLoop, calls=%fused_computation.15.clone.1 | loop fusion | flops 14680064 | bytes 4980800 | tf_op jit(solution)/shard_map/while/body/eval_jaxpr/convert_element_type | solution.py:113
  361.3 1.7 multiply_reduce_fusion.2
  364.2 17.0 %fusion.84 = (bf16[16,1024,64]{1,2,0:T(8,128)(2,1)S(1)}, bf16[16,1024,64]{1,2,0:T(8,128)(2,1)S(1)}) fusion(f32[1024,64]{0,1:T(8,128)S(1)} %get-tuple-element.248, f32[16]{0:T(128)S(1)} %get-tuple-element.249, f32[1024,64]{0,1:T(8,128)S(1)} %get-tuple-element.223, f32[1024,64]{0,1:T(8,128)S(1)} %get-tuple-element.224), kind=kLoop, calls=%fused_computation.15.clone.1 | loop fusion | flops 14680064 | bytes 4980800 | tf_op jit(solution)/shard_map/while/body/eval_jaxpr/convert_element_type | solution.py:113
  384.0 17.0 %fusion.84 = (bf16[16,1024,64]{1,2,0:T(8,128)(2,1)S(1)}, bf16[16,1024,64]{1,2,0:T(8,128)(2,1)S(1)}) fusion(f32[1024,64]{0,1:T(8,128)S(1)} %get-tuple-element.248, f32[16]{0:T(128)S(1)} %get-tuple-element.249, f32[1024,64]{0,1:T(8,128)S(1)} %get-tuple-element.223, f32[1024,64]{0,1:T(8,128)S(1)} %get-tuple-element.224), kind=kLoop, calls=%fused_computation.15.clone.1 | loop fusion | flops 14680064 | bytes 4980800 | tf_op jit(solution)/shard_map/while/body/eval_jaxpr/convert_element_type | solution.py:113
  401.0 1.7 multiply_reduce_fusion.2
  403.9 17.0 %fusion.84 = (bf16[16,1024,64]{1,2,0:T(8,128)(2,1)S(1)}, bf16[16,1024,64]{1,2,0:T(8,128)(2,1)S(1)}) fusion(f32[1024,64]{0,1:T(8,128)S(1)} %get-tuple-element.248, f32[16]{0:T(128)S(1)} %get-tuple-element.249, f32[1024,64]{0,1:T(8,128)S(1)} %get-tuple-element.223, f32[1024,64]{0,1:T(8,128)S(1)} %get-tuple-element.224), kind=kLoop, calls=%fused_computation.15.clone.1 | loop fusion | flops 14680064 | bytes 4980800 | tf_op jit(solution)/shard_map/while/body/eval_jaxpr/convert_element_type | solution.py:113
  423.7 17.0 %fusion.84 = (bf16[16,1024,64]{1,2,0:T(8,128)(2,1)S(1)}, bf16[16,1024,64]{1,2,0:T(8,128)(2,1)S(1)}) fusion(f32[1024,64]{0,1:T(8,128)S(1)} %get-tuple-element.248, f32[16]{0:T(128)S(1)} %get-tuple-element.249, f32[1024,64]{0,1:T(8,128)S(1)} %get-tuple-element.223, f32[1024,64]{0,1:T(8,128)S(1)} %get-tuple-element.224), kind=kLoop, calls=%fused_computation.15.clone.1 | loop fusion | flops 14680064 | bytes 4980800 | tf_op jit(solution)/shard_map/while/body/eval_jaxpr/convert_element_type | solution.py:113
  440.7 1.7 multiply_reduce_fusion.2
  443.6 17.0 %fusion.84 = (bf16[16,1024,64]{1,2,0:T(8,128)(2,1)S(1)}, bf16[16,1024,64]{1,2,0:T(8,128)(2,1)S(1)}) fusion(f32[1024,64]{0,1:T(8,128)S(1)} %get-tuple-element.248, f32[16]{0:T(128)S(1)} %get-tuple-element.249, f32[1024,64]{0,1:T(8,128)S(1)} %get-tuple-element.223, f32[1024,64]{0,1:T(8,128)S(1)} %get-tuple-element.224), kind=kLoop, calls=%fused_computation.15.clone.1 | loop fusion | flops 14680064 | bytes 4980800 | tf_op jit(solution)/shard_map/while/body/eval_jaxpr/convert_element_type | solution.py:113
  463.4 17.0 %fusion.84 = (bf16[16,1024,64]{1,2,0:T(8,128)(2,1)S(1)}, bf16[16,1024,64]{1,2,0:T(8,128)(2,1)S(1)}) fusion(f32[1024,64]{0,1:T(8,128)S(1)} %get-tuple-element.248, f32[16]{0:T(128)S(1)} %get-tuple-element.249, f32[1024,64]{0,1:T(8,128)S(1)} %get-tuple-element.223, f32[1024,64]{0,1:T(8,128)S(1)} %get-tuple-element.224), kind=kLoop, calls=%fused_computation.15.clone.1 | loop fusion | flops 14680064 | bytes 4980800 | tf_op jit(solution)/shard_map/while/body/eval_jaxpr/convert_element_type | solution.py:113
  480.4 1.7 multiply_reduce_fusion.2
  483.2 17.0 %fusion.84 = (bf16[16,1024,64]{1,2,0:T(8,128)(2,1)S(1)}, bf16[16,1024,64]{1,2,0:T(8,128)(2,1)S(1)}) fusion(f32[1024,64]{0,1:T(8,128)S(1)} %get-tuple-element.248, f32[16]{0:T(128)S(1)} %get-tuple-element.249, f32[1024,64]{0,1:T(8,128)S(1)} %get-tuple-element.223, f32[1024,64]{0,1:T(8,128)S(1)} %get-tuple-element.224), kind=kLoop, calls=%fused_computation.15.clone.1 | loop fusion | flops 14680064 | bytes 4980800 | tf_op jit(solution)/shard_map/while/body/eval_jaxpr/convert_element_type | solution.py:113
  503.1 17.0 %fusion.84 = (bf16[16,1024,64]{1,2,0:T(8,128)(2,1)S(1)}, bf16[16,1024,64]{1,2,0:T(8,128)(2,1)S(1)}) fusion(f32[1024,64]{0,1:T(8,128)S(1)} %get-tuple-element.248, f32[16]{0:T(128)S(1)} %get-tuple-element.249, f32[1024,64]{0,1:T(8,128)S(1)} %get-tuple-element.223, f32[1024,64]{0,1:T(8,128)S(1)} %get-tuple-element.224), kind=kLoop, calls=%fused_computation.15.clone.1 | loop fusion | flops 14680064 | bytes 4980800 | tf_op jit(solution)/shard_map/while/body/eval_jaxpr/convert_element_type | solution.py:113
  520.1 1.7 multiply_reduce_fusion.2
  522.9 17.0 %fusion.84 = (bf16[16,1024,64]{1,2,0:T(8,128)(2,1)S(1)}, bf16[16,1024,64]{1,2,0:T(8,128)(2,1)S(1)}) fusion(f32[1024,64]{0,1:T(8,128)S(1)} %get-tuple-element.248, f32[16]{0:T(128)S(1)} %get-tuple-element.249, f32[1024,64]{0,1:T(8,128)S(1)} %get-tuple-element.223, f32[1024,64]{0,1:T(8,128)S(1)} %get-tuple-element.224), kind=kLoop, calls=%fused_computation.15.clone.1 | loop fusion | flops 14680064 | bytes 4980800 | tf_op jit(solution)/shard_map/while/body/eval_jaxpr/convert_element_type | solution.py:113
  543.3 3.8 reduce.2
  547.2 25.5 %all_to_all.33 = bf16[16,2,8192]{2,1,0:T(2,128)(2,1)S(1)} all-to-all(bf16[16,2,8192]{2,1,0:T(2,128)(2,1)S(1)} %reshape.331), channel_id=1, replica_groups=mesh['grp'=2,'chan'=16] {'chan'}, dimensions={0} | all-to-all | bytes 1048576 | tf_op jit(solution)/shard_map/all_to_all | solution.py:125
  (60 shorter events, 33.9 us)
Async XLA Ops:
  78.3 4.8 copy-start.1
  134.6 7.7 %copy-start = (f32[1024,64]{0,1:T(8,128)S(1)}, f32[1024,64]{0,1:T(8,128)}, u32[]{:S(2)}) copy-start(f32[1024,64]{0,1:T(8,128)} %param.7) | copy-start | bytes 786436
  134.6 48.7 %all-to-all-start = ((bf16[16,2,32768]{2,1,0:T(2,128)(2,1)}), bf16[16,2,32768]{2,1,0:T(2,128)(2,1)S(1)}, u32[]{:S(2)}, u32[]{:S(2)}) async-start(bf16[16,2,32768]{2,1,0:T(2,128)(2,1)} %reshape.329), calls=%async_computation | async-start | bytes 4194304 | tf_op jit(solution)/shard_map/all_to_all | solution.py:85
